TPU v7x, 128 devices: a whole 4x4x4 slice. The times are simulated.
128 devices in a mesh: row: 8 (over x, core), col: 16 (over z, y).
Axes of the slice: x: 4, y: 4, z: 4, core: 2. Of those that a mesh axis runs over, the one named last changes fastest.
Arguments:
- unit_factor: float32 [4, 1024, 2, 2048], P(None, 'row', None, 'col'), may hold values from -0.125 to 0.125
- pivot_inverse: float32 [4, 1024, 2, 2048], P(None, 'row', None, 'col')
- supernode: int32 [32], replicated, may hold values from 0 to 2, never falling along the last dimension, each value on 1 to 16 neighbouring positions
- row_bits: int32 [32, 2], replicated, may hold values 0 or 1
Outputs:
- inverse_blocks: float32 [4, 1024, 2, 2048], P(None, 'row', None, 'col')
Inputs may be any that keep to these rules, and one draw needn't show every extreme that they name: The supernode index never decreases from one block to the next; each supernode has 1 to 16 blocks, one of them exactly 16.
All inputs are finite; a program needn't handle non-finite values.
Results may differ from a plain program's by a relative error of at most 0.0001.
Values sent between devices are 32-bit elements; how exact they have to be, the bound alone decides.
No kernel may reach another device: no remote copies, remote signals or barrier semaphores. Data moves between devices by JAX's collectives and lax.ppermute only.
A program may use at most 128 MiB of HBM per device.

v0:
```python
import jax
import jax.numpy as jnp
from jax import lax
from jax.sharding import PartitionSpec as P


SUPERNODES = 3
PRECISION = lax.Precision.HIGH
COL_STAGES = ((1, 4), (4, 4))


def dot(spec, a, b):
    return jnp.einsum(spec, a, b, precision=PRECISION, preferred_element_type=jnp.float32)


def pp_gather(a, axis, stages):
    n = lax.axis_size(axis)
    me = lax.axis_index(axis)
    out = a[None]
    for stride, count in stages:
        def to(i, d, stride=stride, count=count):
            digit = (i // stride) % count
            return i + (((digit + d) % count) - digit) * stride

        parts = [out] + [lax.ppermute(out, axis, [(i, to(i, d)) for i in range(n)]) for d in range(1, count)]
        out = jnp.concatenate(parts, axis=0)
    src = jnp.arange(n)
    at = jnp.zeros((n,), jnp.int32)
    mult = 1
    for stride, count in stages:
        at = at + ((me // stride - src // stride) % count) * mult
        mult *= count
    return jnp.take(out, at, axis=0)


def shards(unit_factor, pivot_inverse, supernode, row_bits):
    n_row = lax.axis_size("row")
    n_col = lax.axis_size("col")
    brows, width, bcols, _ = unit_factor.shape
    r = lax.axis_index("row")
    q = lax.axis_index("col")

    def rows_of(v):
        return lax.dynamic_index_in_dim(v.reshape(brows, n_row), r, axis=1, keepdims=False)

    def cols_of(v):
        return lax.dynamic_index_in_dim(v.reshape(bcols, n_col), q, axis=1, keepdims=False)

    def mask(a, rm=None, cm=None):
        if rm is not None:
            a = a * rm[:, None, None, None]
        if cm is not None:
            a = a * cm[None, None, :, None]
        return a

    def pack_rows(a):
        return a.reshape((brows // 2, 2) + a.shape[1:]).sum(axis=0)

    def unpack_rows(a, rm):
        full = jnp.concatenate([a] * (brows // 2), axis=0)
        return full * rm.reshape((brows,) + (1,) * (a.ndim - 1))

    def scatter_rows(zp):
        zp = jnp.swapaxes(zp.reshape(n_col // n_row, n_row, width, bcols * width), 0, 1)
        zp = zp.reshape(n_col * width, bcols * width)
        zr = lax.psum_scatter(zp, "row", scatter_dimension=0, tiled=True)
        return zr.reshape(n_col // n_row, width, bcols, width)

    f32 = jnp.float32
    member = [(supernode == s).astype(f32) for s in range(SUPERNODES)]
    struct = [
        jnp.logical_and(supernode > s, jnp.all(row_bits[:, s:] == 1, axis=1)).astype(f32)
        for s in range(SUPERNODES - 1)
    ]

    last = SUPERNODES - 1
    rM2, cM2 = rows_of(member[last]), cols_of(member[last])
    x = mask(pivot_inverse, rM2, cM2)

    S1, M1, S0, M0 = struct[1], member[1], struct[0], member[0]
    rS1, cS1, rM1, cM1 = rows_of(S1), cols_of(S1), rows_of(M1), cols_of(M1)
    rS0, cS0, rM0, cM0 = rows_of(S0), cols_of(S0), rows_of(M0), cols_of(M0)

    xm = mask(x, rS1, cS1)
    xc1 = pack_rows(xm.sum(axis=2))
    uc1 = pack_rows(mask(unit_factor, rS1, cM1).sum(axis=2))
    uc0 = mask(unit_factor, rS0, cM0).sum(axis=2)
    xg = lax.all_gather(xc1, "col", axis=1)
    urow1 = pp_gather(uc1, "col", COL_STAGES)
    urow0 = pp_gather(uc0, "col", COL_STAGES)
    send = jnp.concatenate([uc1, uc0], axis=0)
    pieces = [send] + [lax.ppermute(send, "row", [(i, (i + d) % n_row) for i in range(n_row)]) for d in range(1, n_row)]
    by_shift = jnp.stack(pieces)
    grow = jnp.take(by_shift, (r - jnp.arange(n_row)) % n_row, axis=0)
    ucol1, ucol0 = grow[:, 0:2], grow[:, 2:6]

    s1 = S1.reshape(bcols, n_col).sum(axis=0)
    ueff = jnp.transpose(ucol1, (1, 0, 2, 3)).reshape(n_col, width, width) * s1[:, None, None]
    y = dot("pqax,qxb->pab", xg, ueff)
    yl = mask(unpack_rows(y, rS1)[:, :, None, :], None, cM1)
    x = x - yl
    wc = pack_rows(yl - xm)
    zp = dot("qpax,pacb->qxcb", urow1, wc)
    z1 = scatter_rows(zp)
    x = x + unpack_rows(z1, rM1) + mask(pivot_inverse, rM1, cM1)

    xm = mask(x, rS0, cS0)
    xg = lax.all_gather(xm, "col", axis=2)
    u2 = ucol0.reshape(n_row, bcols, n_col // n_row, width, width)
    u2 = jnp.transpose(u2, (2, 0, 1, 3, 4)).reshape(n_col, bcols, width, width)
    y = dot("taqcx,qcxb->tab", xg, u2)
    yl = mask(y[:, :, None, :], None, cM0)
    x = x - yl
    zp = dot("qtax,tacb->qxcb", urow0, yl - xm)
    x = x + unpack_rows(scatter_rows(zp), rM0) + mask(pivot_inverse, rM0, cM0)
    return x


def solution(mesh):
    in_specs = (P(None, "row", None, "col"), P(None, "row", None, "col"), P(), P())
    out_specs = P(None, "row", None, "col")
    return jax.shard_map(shards, mesh=mesh, in_specs=in_specs, out_specs=out_specs, check_vma=False)
```

profile of v0, /device:TPU:0, one launch (start us, length us, event | category | flops | bytes accessed | tf_op | source)
XLA Modules:
  0.0 297.4 jit_solution(2375676746710420644)
XLA Ops:
  13.5 2.1 collective-permute-start.2
  17.2 2.9 collective-permute-start.8
  29.2 2.0 collective-permute-start.3
  42.2 1.9 collective-permute-start.10
  45.1 3.7 %collective-permute-start.11 = (f32[4,2,128,128]{3,2,1,0:T(8,128)}, f32[4,2,128,128]{3,2,1,0:T(8,128)}, u32[]{:S(2)}, u32[]{:S(2)}) collective-permute-start(f32[4,2,128,128]{3,2,1,0:T(8,128)} %pad_maximum_fusion.1), channel_id=1, source_target_pairs={{0,8},{1,9},{2,10},{3,11},{4,12},{5,13},{6,14},{7,15},{8,0},{9,1},... | collective-permute-start | bytes 1572872 | tf_op jit(solution)/shard_map/ppermute | solution.py:25
  48.8 3.2 %collective-permute-start.12 = (f32[4,2,128,128]{3,2,1,0:T(8,128)}, f32[4,2,128,128]{3,2,1,0:T(8,128)}, u32[]{:S(2)}, u32[]{:S(2)}) collective-permute-start(f32[4,2,128,128]{3,2,1,0:T(8,128)} %pad_maximum_fusion.1), channel_id=1, source_target_pairs={{0,12},{1,13},{2,14},{3,15},{4,0},{5,1},{6,2},{7,3},{8,4},{9,5},{1... | collective-permute-start | bytes 1572872 | tf_op jit(solution)/shard_map/ppermute | solution.py:25
  52.1 5.4 %collective-permute-done.5 = f32[6,128,128]{2,1,0:T(8,128)S(1)} collective-permute-done((f32[6,128,128]{2,1,0:T(8,128)}, f32[6,128,128]{2,1,0:T(8,128)S(1)}, u32[]{:S(2)}, u32[]{:S(2)}) %collective-permute-start.5) | collective-permute-done | bytes 393248 | tf_op jit(solution)/shard_map/ppermute | solution.py:92
  57.5 3.2 %collective-permute-done.6 = f32[6,128,128]{2,1,0:T(8,128)S(1)} collective-permute-done((f32[6,128,128]{2,1,0:T(8,128)}, f32[6,128,128]{2,1,0:T(8,128)S(1)}, u32[]{:S(2)}, u32[]{:S(2)}) %collective-permute-start.6) | collective-permute-done | bytes 393248 | tf_op jit(solution)/shard_map/ppermute | solution.py:92
  60.8 2.5 gather_fusion
  63.3 2.2 broadcast_select_fusion
  67.3 1.9 constant_dynamic-update-slice_fusion.2
  69.2 8.1 %collective-permute-done.11 = f32[4,2,128,128]{3,2,1,0:T(8,128)} collective-permute-done((f32[4,2,128,128]{3,2,1,0:T(8,128)}, f32[4,2,128,128]{3,2,1,0:T(8,128)}, u32[]{:S(2)}, u32[]{:S(2)}) %collective-permute-start.11) | collective-permute-done | bytes 524320 | tf_op jit(solution)/shard_map/ppermute | solution.py:25
  77.4 1.9 constant_dynamic-update-slice_fusion.1
  79.5 1.9 constant_dynamic-update-slice_fusion
  81.4 3.7 %gather_fusion.1 = f32[16,2,128,128]{3,2,1,0:T(8,128)} fusion(f32[16,2,128,128]{3,2,1,0:T(8,128)} %constant_dynamic-update-slice_fusion, s32[1024]{0:T(1024)} %pad_clamp_fusion), kind=kCustom, calls=%fused_computation.1 | custom fusion | bytes 4194368 | tf_op jit(solution)/shard_map/jit(_take)/gather | solution.py:33
  85.1 3.3 %broadcast_select_fusion.1 = f32[16,2,128,128]{3,2,1,0:T(8,128)} fusion(f32[16,2,128,128]{3,2,1,0:T(8,128)} %gather_fusion.1, pred[16]{0:T(512)(128)(4,1)S(1)} %copy-done.22), kind=kLoop, calls=%fused_computation.16 | loop fusion | flops 524288 | bytes 4194320 | tf_op jit(solution)/shard_map/jit(_take)/select_n | solution.py:33
  88.4 2.9 convolution_bitcast_fusion.2
  96.0 3.4 %convolution_bitcast_fusion = f32[8,2,128,256]{3,2,0,1:T(8,128)S(1)} fusion(f32[2,8,128,128,2]{2,3,4,1,0:T(8,128)} %bitcast.100, f32[256,128,2,1,1]{1,0,2,4,3:T(8,128)} %bitcast.115), kind=kOutput, calls=%fused_computation.8 | convolution fusion | flops 805306368 | bytes 4456448 | tf_op jit(solution)/shard_map/qpax,pacb->qxcb/dot_general | solution.py:13
  101.6 33.7 %reduce-scatter.3.cloned.1.call-done = f32[256,256]{1,0:T(8,128)} async-done(((f32[2048,256]{1,0:T(8,128)}), f32[256,256]{1,0:T(8,128)}) %reduce-scatter.3.cloned.1.call-update) | async-done | bytes 262160 | tf_op jit(solution)/shard_map/reduce_scatter | solution.py:66
  138.8 2.2 multiply_multiply_fusion
  142.6 2.7 collective-permute-start.14
  146.6 4.8 %collective-permute-done.13 = f32[1,4,128,128]{3,2,1,0:T(8,128)S(1)} collective-permute-done((f32[1,4,128,128]{3,2,1,0:T(8,128)S(1)}, f32[1,4,128,128]{3,2,1,0:T(8,128)S(1)}, u32[]{:S(2)}, u32[]{:S(2)}) %collective-permute-start.13) | collective-permute-done | bytes 262176 | tf_op jit(solution)/shard_map/ppermute | solution.py:25
  151.4 2.8 collective-permute-done.14
  155.8 2.1 collective-permute-start.16
  157.9 2.8 collective-permute-start.17
  165.3 22.7 %collective-permute-done.16 = f32[4,4,128,128]{3,2,1,0:T(8,128)S(1)} collective-permute-done((f32[4,4,128,128]{3,2,1,0:T(8,128)S(1)}, f32[4,4,128,128]{3,2,1,0:T(8,128)S(1)}, u32[]{:S(2)}, u32[]{:S(2)}) %collective-permute-start.16) | collective-permute-done | bytes 1048608 | tf_op jit(solution)/shard_map/ppermute | solution.py:25
  189.0 27.8 %collective-permute-done.17 = f32[4,4,128,128]{3,2,1,0:T(8,128)S(1)} collective-permute-done((f32[4,4,128,128]{3,2,1,0:T(8,128)S(1)}, f32[4,4,128,128]{3,2,1,0:T(8,128)S(1)}, u32[]{:S(2)}, u32[]{:S(2)}) %collective-permute-start.17) | collective-permute-done | bytes 1048608 | tf_op jit(solution)/shard_map/ppermute | solution.py:25
  219.0 5.2 %gather_fusion.2 = f32[16,4,128,128]{3,2,1,0:T(8,128)} fusion(f32[16,4,128,128]{3,2,1,0:T(8,128)} %constant_dynamic-update-slice_fusion.7, s32[1024]{0:T(1024)} %pad_clamp_fusion), kind=kCustom, calls=%fused_computation.2 | custom fusion | bytes 8388672 | tf_op jit(solution)/shard_map/jit(_take)/gather | solution.py:33
  224.1 18.0 %all-gather.7.cloned.1.call-done = f32[4,128,32,128]{3,1,2,0:T(8,128)} async-done(((f32[4,128,2,128]{3,1,2,0:T(8,128)}), f32[4,128,32,128]{3,1,2,0:T(8,128)}) %all-gather.7.cloned.1.call-update) | async-done | bytes 8388624 | tf_op jit(solution)/shard_map/all_gather | solution.py:108
  242.2 6.0 %convolution_bitcast_fusion.1 = f32[4,128,128]{2,1,0:T(8,128)S(1)} fusion(f32[4,128,16,2,128]{4,1,3,2,0:T(8,128)} %bitcast.98, f32[16,2,128,128,1]{3,2,1,0,4:T(8,128)S(1)} %bitcast.103), kind=kOutput, calls=%fused_computation.10 | convolution fusion | flops 1610612736 | bytes 10747904 | tf_op jit(solution)/shard_map/taqcx,qcxb->tab/dot_general | solution.py:13
  248.2 2.2 fusion
  252.6 35.5 %reduce-scatter.5.cloned.1.call-done = f32[256,256]{1,0:T(8,128)} async-done(((f32[2048,256]{1,0:T(8,128)}), f32[256,256]{1,0:T(8,128)}) %reduce-scatter.5.cloned.1.call-update) | async-done | bytes 262160 | tf_op jit(solution)/shard_map/reduce_scatter | solution.py:66
  (147 shorter events, 58.8 us)
Async XLA Ops:
  6.5 81.9 %all-gather.5.cloned.1.call-start = ((), (), s32[]{:S(2)}) async-start(), calls=%async_computation.4 | async-start | bytes 2228224 | tf_op jit(solution)/shard_map/all_gather | solution.py:88
  11.9 24.1 %collective-permute-start = (f32[6,128,128]{2,1,0:T(8,128)}, f32[6,128,128]{2,1,0:T(8,128)}, u32[]{:S(2)}, u32[]{:S(2)}) collective-permute-start(f32[6,128,128]{2,1,0:T(8,128)} %pad_maximum_fusion.2), channel_id=1, source_target_pairs={{0,16},{16,32},{32,48},{48,64},{64,80},{80,96},{96,112},{112,0},{1... | collective-permute-start | bytes 1179656 | tf_op jit(solution)/shard_map/ppermute | solution.py:92
  11.9 26.6 %collective-permute-start.1 = (f32[6,128,128]{2,1,0:T(8,128)}, f32[6,128,128]{2,1,0:T(8,128)}, u32[]{:S(2)}, u32[]{:S(2)}) collective-permute-start(f32[6,128,128]{2,1,0:T(8,128)} %pad_maximum_fusion.2), channel_id=1, source_target_pairs={{0,32},{16,48},{32,64},{48,80},{64,96},{80,112},{96,0},{112,16},{1... | collective-permute-start | bytes 1179656 | tf_op jit(solution)/shard_map/ppermute | solution.py:92
  13.5 28.7 %collective-permute-start.2 = (f32[6,128,128]{2,1,0:T(8,128)}, f32[6,128,128]{2,1,0:T(8,128)}, u32[]{:S(2)}, u32[]{:S(2)}) collective-permute-start(f32[6,128,128]{2,1,0:T(8,128)} %pad_maximum_fusion.2), channel_id=1, source_target_pairs={{0,48},{16,64},{32,80},{48,96},{64,112},{80,0},{96,16},{112,32},{1... | collective-permute-start | bytes 1179656 | tf_op jit(solution)/shard_map/ppermute | solution.py:92
  15.6 10.7 %collective-permute-start.7 = (f32[1,2,128,128]{3,2,1,0:T(8,128)S(1)}, f32[1,2,128,128]{3,2,1,0:T(8,128)}, u32[]{:S(2)}, u32[]{:S(2)}) collective-permute-start(f32[1,2,128,128]{3,2,1,0:T(8,128)S(1)} %bitcast.109), channel_id=1, source_target_pairs={{0,1},{1,2},{2,3},{3,0},{4,5},{5,6},{6,7},{7,4},{8,9},{9,10},{10,1... | collective-permute-start | bytes 393224 | tf_op jit(solution)/shard_map/ppermute | solution.py:25
  17.2 12.0 %collective-permute-start.8 = (f32[1,2,128,128]{3,2,1,0:T(8,128)S(1)}, f32[1,2,128,128]{3,2,1,0:T(8,128)}, u32[]{:S(2)}, u32[]{:S(2)}) collective-permute-start(f32[1,2,128,128]{3,2,1,0:T(8,128)S(1)} %bitcast.110), channel_id=1, source_target_pairs={{0,2},{1,3},{2,0},{3,1},{4,6},{5,7},{6,4},{7,5},{8,10},{9,11},{10,... | collective-permute-start | bytes 393224 | tf_op jit(solution)/shard_map/ppermute | solution.py:25
  20.8 114.5 %reduce-scatter.3.cloned.1.call-start = ((), (), s32[]{:S(2)}) async-start(), calls=%async_computation.2 | async-start | bytes 2359296 | tf_op jit(solution)/shard_map/reduce_scatter | solution.py:66
  26.3 6.5 %collective-permute-start.9 = (f32[1,2,128,128]{3,2,1,0:T(8,128)S(1)}, f32[1,2,128,128]{3,2,1,0:T(8,128)S(1)}, u32[]{:S(2)}, u32[]{:S(2)}) collective-permute-start(f32[1,2,128,128]{3,2,1,0:T(8,128)S(1)} %bitcast.111), channel_id=1, source_target_pairs={{0,3},{1,0},{2,1},{3,2},{4,7},{5,4},{6,5},{7,6},{8,11},{9,8},{10,9... | collective-permute-start | bytes 393224 | tf_op jit(solution)/shard_map/ppermute | solution.py:25
  29.2 15.9 %collective-permute-start.3 = (f32[6,128,128]{2,1,0:T(8,128)}, f32[6,128,128]{2,1,0:T(8,128)S(1)}, u32[]{:S(2)}, u32[]{:S(2)}) collective-permute-start(f32[6,128,128]{2,1,0:T(8,128)} %pad_maximum_fusion.2), channel_id=1, source_target_pairs={{0,64},{16,80},{32,96},{48,112},{64,0},{80,16},{96,32},{112,48},{1... | collective-permute-start | bytes 1179656 | tf_op jit(solution)/shard_map/ppermute | solution.py:92
  32.8 16.0 %collective-permute-start.4 = (f32[6,128,128]{2,1,0:T(8,128)}, f32[6,128,128]{2,1,0:T(8,128)S(1)}, u32[]{:S(2)}, u32[]{:S(2)}) collective-permute-start(f32[6,128,128]{2,1,0:T(8,128)} %pad_maximum_fusion.2), channel_id=1, source_target_pairs={{0,80},{16,96},{32,112},{48,0},{64,16},{80,32},{96,48},{112,64},{1... | collective-permute-start | bytes 1179656 | tf_op jit(solution)/shard_map/ppermute | solution.py:92
  36.0 21.5 %collective-permute-start.5 = (f32[6,128,128]{2,1,0:T(8,128)}, f32[6,128,128]{2,1,0:T(8,128)S(1)}, u32[]{:S(2)}, u32[]{:S(2)}) collective-permute-start(f32[6,128,128]{2,1,0:T(8,128)} %pad_maximum_fusion.2), channel_id=1, source_target_pairs={{0,96},{16,112},{32,0},{48,16},{64,32},{80,48},{96,64},{112,80},{1... | collective-permute-start | bytes 1179656 | tf_op jit(solution)/shard_map/ppermute | solution.py:92
  38.5 22.2 %collective-permute-start.6 = (f32[6,128,128]{2,1,0:T(8,128)}, f32[6,128,128]{2,1,0:T(8,128)S(1)}, u32[]{:S(2)}, u32[]{:S(2)}) collective-permute-start(f32[6,128,128]{2,1,0:T(8,128)} %pad_maximum_fusion.2), channel_id=1, source_target_pairs={{0,112},{16,0},{32,16},{48,32},{64,48},{80,64},{96,80},{112,96},{1... | collective-permute-start | bytes 1179656 | tf_op jit(solution)/shard_map/ppermute | solution.py:92
  42.2 25.1 %collective-permute-start.10 = (f32[4,2,128,128]{3,2,1,0:T(8,128)}, f32[4,2,128,128]{3,2,1,0:T(8,128)}, u32[]{:S(2)}, u32[]{:S(2)}) collective-permute-start(f32[4,2,128,128]{3,2,1,0:T(8,128)} %pad_maximum_fusion.1), channel_id=1, source_target_pairs={{0,4},{1,5},{2,6},{3,7},{4,8},{5,9},{6,10},{7,11},{8,12},{9,13},{1... | collective-permute-start | bytes 1572872 | tf_op jit(solution)/shard_map/ppermute | solution.py:25
  45.1 32.2 %collective-permute-start.11 = (f32[4,2,128,128]{3,2,1,0:T(8,128)}, f32[4,2,128,128]{3,2,1,0:T(8,128)}, u32[]{:S(2)}, u32[]{:S(2)}) collective-permute-start(f32[4,2,128,128]{3,2,1,0:T(8,128)} %pad_maximum_fusion.1), channel_id=1, source_target_pairs={{0,8},{1,9},{2,10},{3,11},{4,12},{5,13},{6,14},{7,15},{8,0},{9,1},... | collective-permute-start | bytes 1572872 | tf_op jit(solution)/shard_map/ppermute | solution.py:25
  48.8 30.6 %collective-permute-start.12 = (f32[4,2,128,128]{3,2,1,0:T(8,128)}, f32[4,2,128,128]{3,2,1,0:T(8,128)}, u32[]{:S(2)}, u32[]{:S(2)}) collective-permute-start(f32[4,2,128,128]{3,2,1,0:T(8,128)} %pad_maximum_fusion.1), channel_id=1, source_target_pairs={{0,12},{1,13},{2,14},{3,15},{4,0},{5,1},{6,2},{7,3},{8,4},{9,5},{1... | collective-permute-start | bytes 1572872 | tf_op jit(solution)/shard_map/ppermute | solution.py:25
  69.2 15.9 %copy-start.22 = (pred[16]{0:T(512)(128)(4,1)S(1)}, pred[16]{0:T(512)(128)(4,1)}, u32[]{:S(2)}) copy-start(pred[16]{0:T(512)(128)(4,1)} %compare_and_fusion) | copy-start | bytes 52
  85.1 6.3 %copy-start.11 = (f32[2]{0:T(128)S(1)}, f32[2]{0:T(128)}, u32[]{:S(2)}) copy-start(f32[2]{0:T(128)} %copy-done.10) | copy-start | bytes 28
  99.5 39.3 %copy-start.13 = (f32[4]{0:T(128)S(1)}, f32[4]{0:T(128)}, u32[]{:S(2)}) copy-start(f32[4]{0:T(128)} %copy-done.12) | copy-start | bytes 52
  101.0 141.1 %all-gather.7.cloned.1.call-start = ((), (), s32[]{:S(2)}) async-start(), calls=%async_computation.5 | async-start | bytes 8912896 | tf_op jit(solution)/shard_map/all_gather | solution.py:108
  141.0 147.2 %reduce-scatter.5.cloned.1.call-start = ((), (), s32[]{:S(2)}) async-start(), calls=%async_computation.3 | async-start | bytes 2359296 | tf_op jit(solution)/shard_map/reduce_scatter | solution.py:66
  141.0 10.4 %collective-permute-start.13 = (f32[1,4,128,128]{3,2,1,0:T(8,128)S(1)}, f32[1,4,128,128]{3,2,1,0:T(8,128)S(1)}, u32[]{:S(2)}, u32[]{:S(2)}) collective-permute-start(f32[1,4,128,128]{3,2,1,0:T(8,128)S(1)} %bitcast.105), channel_id=1, source_target_pairs={{0,1},{1,2},{2,3},{3,0},{4,5},{5,6},{6,7},{7,4},{8,9},{9,10},{10,1... | collective-permute-start | bytes 786440 | tf_op jit(solution)/shard_map/ppermute | solution.py:25
  142.6 11.7 %collective-permute-start.14 = (f32[1,4,128,128]{3,2,1,0:T(8,128)S(1)}, f32[1,4,128,128]{3,2,1,0:T(8,128)S(1)}, u32[]{:S(2)}, u32[]{:S(2)}) collective-permute-start(f32[1,4,128,128]{3,2,1,0:T(8,128)S(1)} %bitcast.106), channel_id=1, source_target_pairs={{0,2},{1,3},{2,0},{3,1},{4,6},{5,7},{6,4},{7,5},{8,10},{9,11},{10,... | collective-permute-start | bytes 786440 | tf_op jit(solution)/shard_map/ppermute | solution.py:25
  145.3 10.4 %collective-permute-start.15 = (f32[1,4,128,128]{3,2,1,0:T(8,128)S(1)}, f32[1,4,128,128]{3,2,1,0:T(8,128)S(1)}, u32[]{:S(2)}, u32[]{:S(2)}) collective-permute-start(f32[1,4,128,128]{3,2,1,0:T(8,128)S(1)} %bitcast.107), channel_id=1, source_target_pairs={{0,3},{1,0},{2,1},{3,2},{4,7},{5,4},{6,5},{7,6},{8,11},{9,8},{10,9... | collective-permute-start | bytes 786440 | tf_op jit(solution)/shard_map/ppermute | solution.py:25
  155.8 32.2 %collective-permute-start.16 = (f32[4,4,128,128]{3,2,1,0:T(8,128)S(1)}, f32[4,4,128,128]{3,2,1,0:T(8,128)S(1)}, u32[]{:S(2)}, u32[]{:S(2)}) collective-permute-start(f32[4,4,128,128]{3,2,1,0:T(8,128)S(1)} %pad_maximum_fusion), channel_id=1, source_target_pairs={{0,4},{1,5},{2,6},{3,7},{4,8},{5,9},{6,10},{7,11},{8,12},{9,13},{1... | collective-permute-start | bytes 3145736 | tf_op jit(solution)/shard_map/ppermute | solution.py:25
  157.9 58.9 %collective-permute-start.17 = (f32[4,4,128,128]{3,2,1,0:T(8,128)S(1)}, f32[4,4,128,128]{3,2,1,0:T(8,128)S(1)}, u32[]{:S(2)}, u32[]{:S(2)}) collective-permute-start(f32[4,4,128,128]{3,2,1,0:T(8,128)S(1)} %pad_maximum_fusion), channel_id=1, source_target_pairs={{0,8},{1,9},{2,10},{3,11},{4,12},{5,13},{6,14},{7,15},{8,0},{9,1},... | collective-permute-start | bytes 3145736 | tf_op jit(solution)/shard_map/ppermute | solution.py:25
  160.7 57.2 %collective-permute-start.18 = (f32[4,4,128,128]{3,2,1,0:T(8,128)S(1)}, f32[4,4,128,128]{3,2,1,0:T(8,128)S(1)}, u32[]{:S(2)}, u32[]{:S(2)}) collective-permute-start(f32[4,4,128,128]{3,2,1,0:T(8,128)S(1)} %pad_maximum_fusion), channel_id=1, source_target_pairs={{0,12},{1,13},{2,14},{3,15},{4,0},{5,1},{6,2},{7,3},{8,4},{9,5},{1... | collective-permute-start | bytes 3145736 | tf_op jit(solution)/shard_map/ppermute | solution.py:25
  242.1 6.0 %copy-start = (f32[16,4,128,128]{3,2,1,0:T(8,128)S(1)}, f32[16,4,128,128]{3,2,1,0:T(8,128)}, u32[]{:S(2)}) copy-start(f32[16,4,128,128]{3,2,1,0:T(8,128)} %gather_fusion.2) | copy-start | bytes 12582916
  242.2 6.0 %copy-start.3 = (f32[4,128,2,128]{3,1,2,0:T(8,128)S(1)}, f32[4,128,2,128]{3,1,2,0:T(8,128)}, u32[]{:S(2)}) copy-start(f32[4,128,2,128]{3,1,2,0:T(8,128)} %multiply_multiply_fusion) | copy-start | bytes 1572868
  242.2 6.1 %copy-start.9 = (f32[2]{0:T(128)S(1)}, f32[2]{0:T(128)}, u32[]{:S(2)}) copy-start(f32[2]{0:T(128)} %copy-done.8) | copy-start | bytes 28
  250.4 38.9 %copy-start.2 = (f32[4,128,2,128]{3,2,1,0:T(2,128)S(1)}, f32[4,128,2,128]{3,2,1,0:T(2,128)}, u32[]{:S(2)}) copy-start(f32[4,128,2,128]{3,2,1,0:T(2,128)} %param.5) | copy-start | bytes 1572868
  250.4 38.9 %copy-start.5 = (f32[4,128,128]{2,1,0:T(8,128)S(1)}, f32[4,128,128]{2,1,0:T(8,128)}, u32[]{:S(2)}) copy-start(f32[4,128,128]{2,1,0:T(8,128)} %copy-done.4) | copy-start | bytes 786436
  250.4 38.9 %copy-start.7 = (f32[2,128,2,128]{3,1,2,0:T(8,128)S(1)}, f32[2,128,2,128]{3,1,2,0:T(8,128)}, u32[]{:S(2)}) copy-start(f32[2,128,2,128]{3,1,2,0:T(8,128)} %copy-done.6) | copy-start | bytes 786436
  (15 other events, 23.7 us)
Sparse Core Ops, SparseCore 0:
  20.9 57.4 all-gather.4
  101.2 34.1 reduce-scatter.2
  141.1 101.0 all-gather.6
  252.4 35.6 reduce-scatter.4
where the time goes:
time: 298 us; the launch traced here: 297 us
  waiting for transfers between devices  166 us (56%)
  local copies, waits for them, and re-layouts  45.2 us (15%)
  starting transfers between devices  35.2 us (12%)
  other arithmetic  23.1 us (8%)
  matrix products  14.5 us (5%)
  between operations  13.6 us (5%)
    reduce_scatter x2, waiting for transfers between devices, scatter_rows(): zr = lax.psum_scatter(zp, 'row', scatter_dimension=0, tiled=True)  69.2 us
    ppermute x12, waiting for transfers between devices, pp_gather(): lax.ppermute(out, axis, [(i, to(i, d)) for i in range(n)])  68 us
    ppermute x12, starting transfers between devices, pp_gather(): lax.ppermute(out, axis, [(i, to(i, d)) for i in range(n)])  26.4 us
    all_gather x1, waiting for transfers between devices, shards(): xg = lax.all_gather(xm, 'col', axis=2)  18 us
    unnamed x66, local copies, waits for them, and re-layouts  17.8 us
    dot_general x4, matrix products, dot(): jnp.einsum(spec, a, b, precision=PRECISION, preferred_element_type=jnp.fl...  14.5 us
    ppermute x7, waiting for transfers between devices, shards(): lax.ppermute(send, 'row', [(i, (i + d) % n_row) for i in range(n_row)])  10.5 us
    gather x2, local copies, waits for them, and re-layouts, pp_gather(): return jnp.take(out, at, axis=0)  8.92 us
  transfers between devices with their start and end apart: 23, of which 13 were waited for; matrix products, arithmetic and copies ran while one was open for 16% of the time, Pallas kernels for 0%

commit v1 on v0

--- a/solution.py
+++ b/solution.py
@@ -85,13 +85,14 @@
     xc1 = pack_rows(xm.sum(axis=2))
     uc1 = pack_rows(mask(unit_factor, rS1, cM1).sum(axis=2))
     uc0 = mask(unit_factor, rS0, cM0).sum(axis=2)
-    xg = lax.all_gather(xc1, "col", axis=1)
-    urow1 = pp_gather(uc1, "col", COL_STAGES)
+    u1t = jnp.transpose(uc1, (2, 0, 1)).reshape(2, width, width)
+    gcol = lax.all_gather(jnp.concatenate([xc1, u1t], axis=0), "col", axis=1)
     urow0 = pp_gather(uc0, "col", COL_STAGES)
     send = jnp.concatenate([uc1, uc0], axis=0)
     pieces = [send] + [lax.ppermute(send, "row", [(i, (i + d) % n_row) for i in range(n_row)]) for d in range(1, n_row)]
     by_shift = jnp.stack(pieces)
     grow = jnp.take(by_shift, (r - jnp.arange(n_row)) % n_row, axis=0)
+    xg, urow1 = gcol[0:2], gcol[2:4]
     ucol1, ucol0 = grow[:, 0:2], grow[:, 2:6]
 
     s1 = S1.reshape(bcols, n_col).sum(axis=0)
@@ -100,7 +101,8 @@
     yl = mask(unpack_rows(y, rS1)[:, :, None, :], None, cM1)
     x = x - yl
     wc = pack_rows(yl - xm)
-    zp = dot("qpax,pacb->qxcb", urow1, wc)
+    u1m = jnp.transpose(urow1, (1, 0, 2, 3)).reshape(n_col * width, 2 * width)
+    zp = dot("ij,jk->ik", u1m, wc.reshape(2 * width, bcols * width)).reshape(n_col, width, bcols, width)
     z1 = scatter_rows(zp)
     x = x + unpack_rows(z1, rM1) + mask(pivot_inverse, rM1, cM1)
 

time: 298 us -> 284 us (0.953)
  starting transfers between devices: 35.2 us -> 28.2 us
  other arithmetic: 23.1 us -> 16.3 us
  local copies, waits for them, and re-layouts: 45.2 us -> 49 us
    ppermute x12 -> x6, starting transfers between devices: 26.4 us -> 12 us  [pp_gather(): lax.ppermute(out, axis, [(i, to(i, d)) for i in range(n)])]
    ppermute x12 -> x6, waiting for transfers between devices: 68 us -> 55.6 us  [pp_gather(): lax.ppermute(out, axis, [(i, to(i, d)) for i in range(n)])]
    all_gather x1, waiting for transfers between devices: 0.01 us -> 8.51 us  [shards(): gcol = lax.all_gather(jnp.concatenate([xc1, u1t], axis=0), 'col', axis=1)]
    ppermute x7, starting transfers between devices: 8.72 us -> 16.1 us  [shards(): lax.ppermute(send, 'row', [(i, (i + d) % n_row) for i in range(n_row)])]
    slice x0 -> x2, local copies, waits for them, and re-layouts: none -> 7.12 us  [shards(): xg, urow1 = (gcol[0:2], gcol[2:4])]
    ppermute x7, waiting for transfers between devices: 10.5 us -> 15.1 us  [shards(): lax.ppermute(send, 'row', [(i, (i + d) % n_row) for i in range(n_row)])]
    gather x2 -> x1, local copies, waits for them, and re-layouts: 8.92 us -> 5.05 us  [pp_gather(): return jnp.take(out, at, axis=0)]
    select_n x2 -> x1, other arithmetic: 3.29 us -> 0.02 us  [pp_gather(): return jnp.take(out, at, axis=0)]
  transfers between devices with their start and end apart: 23 -> 17, of which waited for: 13 -> 14; matrix products, arithmetic and copies ran while one was open for 16% -> 11% of each run, Pallas kernels for 0% -> 0%
where the time goes in v1:
time: 284 us
  waiting for transfers between devices  165 us (58%)
  local copies, waits for them, and re-layouts  49 us (17%)
  starting transfers between devices  28.2 us (10%)
  other arithmetic  16.3 us (6%)
  between operations  13.6 us (5%)
  matrix products  11.7 us (4%)
    reduce_scatter x2, waiting for transfers between devices, scatter_rows(): zr = lax.psum_scatter(zp, 'row', scatter_dimension=0, tiled=True)  68.6 us
    ppermute x6, waiting for transfers between devices, pp_gather(): lax.ppermute(out, axis, [(i, to(i, d)) for i in range(n)])  55.6 us
    all_gather x1, waiting for transfers between devices, shards(): xg = lax.all_gather(xm, 'col', axis=2)  16.8 us
    ppermute x7, starting transfers between devices, shards(): lax.ppermute(send, 'row', [(i, (i + d) % n_row) for i in range(n_row)])  16.1 us
    unnamed x64, local copies, waits for them, and re-layouts  15.4 us
    ppermute x7, waiting for transfers between devices, shards(): lax.ppermute(send, 'row', [(i, (i + d) % n_row) for i in range(n_row)])  15.1 us
    ppermute x6, starting transfers between devices, pp_gather(): lax.ppermute(out, axis, [(i, to(i, d)) for i in range(n)])  12 us
    dot_general x4, matrix products, dot(): jnp.einsum(spec, a, b, precision=PRECISION, preferred_element_type=jnp.fl...  11.7 us
  transfers between devices with their start and end apart: 17, of which 14 were waited for; matrix products, arithmetic and copies ran while one was open for 11% of the time, Pallas kernels for 0%

profile of v1, /device:TPU:0, one launch (start us, length us, event | category | flops | bytes accessed | tf_op | source)
XLA Modules:
  0.0 283.6 jit_solution(3908570699693509064)
XLA Ops:
  14.3 2.1 collective-permute-start.2
  16.5 2.0 collective-permute-start.3
  21.7 3.4 %collective-permute-done = f32[6,128,128]{2,1,0:T(8,128)} collective-permute-done((f32[6,128,128]{2,1,0:T(8,128)}, f32[6,128,128]{2,1,0:T(8,128)}, u32[]{:S(2)}, u32[]{:S(2)}) %collective-permute-start) | collective-permute-done | bytes 393248 | tf_op jit(solution)/shard_map/ppermute | solution.py:92
  27.8 7.1 %collective-permute-start.6 = (f32[6,128,128]{2,1,0:T(8,128)}, f32[6,128,128]{2,1,0:T(8,128)S(1)}, u32[]{:S(2)}, u32[]{:S(2)}) collective-permute-start(f32[6,128,128]{2,1,0:T(8,128)} %pad_maximum_fusion.1), channel_id=1, source_target_pairs={{0,112},{16,0},{32,16},{48,32},{64,48},{80,64},{96,80},{112,96},{1... | collective-permute-start | bytes 1179656 | tf_op jit(solution)/shard_map/ppermute | solution.py:92
  35.9 7.1 %collective-permute-done.2 = f32[6,128,128]{2,1,0:T(8,128)} collective-permute-done((f32[6,128,128]{2,1,0:T(8,128)}, f32[6,128,128]{2,1,0:T(8,128)}, u32[]{:S(2)}, u32[]{:S(2)}) %collective-permute-start.2) | collective-permute-done | bytes 393248 | tf_op jit(solution)/shard_map/ppermute | solution.py:92
  45.2 3.6 %collective-permute-done.4 = f32[6,128,128]{2,1,0:T(8,128)} collective-permute-done((f32[6,128,128]{2,1,0:T(8,128)}, f32[6,128,128]{2,1,0:T(8,128)}, u32[]{:S(2)}, u32[]{:S(2)}) %collective-permute-start.4) | collective-permute-done | bytes 393248 | tf_op jit(solution)/shard_map/ppermute | solution.py:92
  50.8 2.5 gather_fusion
  53.4 2.4 broadcast_select_fusion
  57.6 8.5 %all-gather.5.cloned.1.call-done = f32[4,2048,128]{2,1,0:T(8,128)} async-done(((f32[4,128,128]{2,1,0:T(8,128)}), f32[4,2048,128]{2,1,0:T(8,128)}) %all-gather.5.cloned.1.call-update) | async-done | bytes 4194320 | tf_op jit(solution)/shard_map/all_gather | solution.py:89
  66.1 4.0 %fusion.42 = (f32[2,2048,128]{2,1,0:T(8,128)S(1)}, f32[2,2048,128]{2,1,0:T(8,128)}) fusion(f32[4,2048,128]{2,1,0:T(8,128)} %all-gather.5.cloned.1.call-done), kind=kLoop, calls=%fused_computation.130 | loop fusion | bytes 8388608 | tf_op jit(solution)/shard_map/slice | solution.py:95
  72.1 1.8 reduce_sum.69
  73.9 1.9 copy.83
  75.8 1.9 reshape.344
  77.7 3.2 %copy.119 = f32[2,16,128,128]{3,2,0,1:T(8,128)} copy(f32[2,16,128,128]{3,2,1,0:T(8,128)} %bitcast.100) | data formatting | bytes 4194304 | tf_op jit(solution)/shard_map/slice | solution.py:95
  80.8 2.8 %dot_general.15 = f32[2,8,128,256]{3,2,1,0:T(8,128)} reshape(f32[16,2,128,128]{3,2,1,0:T(8,128)} %bitcast.97) | data formatting | bytes 4194304 | tf_op jit(solution)/shard_map/ij,jk->ik/dot_general | solution.py:13
  83.7 2.6 convolution_bitcast_fusion
  88.4 33.0 %reduce-scatter.3.cloned.1.call-done = f32[256,256]{1,0:T(8,128)} async-done(((f32[2048,256]{1,0:T(8,128)}), f32[256,256]{1,0:T(8,128)}) %reduce-scatter.3.cloned.1.call-update) | async-done | bytes 262160 | tf_op jit(solution)/shard_map/reduce_scatter | solution.py:66
  124.9 2.2 multiply_multiply_fusion
  128.6 2.8 collective-permute-start.8
  132.8 4.8 %collective-permute-done.7 = f32[1,4,128,128]{3,2,1,0:T(8,128)S(1)} collective-permute-done((f32[1,4,128,128]{3,2,1,0:T(8,128)S(1)}, f32[1,4,128,128]{3,2,1,0:T(8,128)S(1)}, u32[]{:S(2)}, u32[]{:S(2)}) %collective-permute-start.7) | collective-permute-done | bytes 262176 | tf_op jit(solution)/shard_map/ppermute | solution.py:25
  137.5 2.8 collective-permute-done.8
  142.9 1.9 collective-permute-start.10
  144.7 2.9 %collective-permute-start.11 = (f32[4,4,128,128]{3,2,1,0:T(8,128)}, f32[4,4,128,128]{3,2,1,0:T(8,128)S(1)}, u32[]{:S(2)}, u32[]{:S(2)}) collective-permute-start(f32[4,4,128,128]{3,2,1,0:T(8,128)} %pad_maximum_fusion), channel_id=1, source_target_pairs={{0,8},{1,9},{2,10},{3,11},{4,12},{5,13},{6,14},{7,15},{8,0},{9,1},... | collective-permute-start | bytes 3145736 | tf_op jit(solution)/shard_map/ppermute | solution.py:25
  155.3 19.2 %collective-permute-done.10 = f32[4,4,128,128]{3,2,1,0:T(8,128)} collective-permute-done((f32[4,4,128,128]{3,2,1,0:T(8,128)}, f32[4,4,128,128]{3,2,1,0:T(8,128)}, u32[]{:S(2)}, u32[]{:S(2)}) %collective-permute-start.10) | collective-permute-done | bytes 1048608 | tf_op jit(solution)/shard_map/ppermute | solution.py:25
  174.5 2.3 constant_dynamic-update-slice_fusion.2
  176.8 27.5 %collective-permute-done.11 = f32[4,4,128,128]{3,2,1,0:T(8,128)S(1)} collective-permute-done((f32[4,4,128,128]{3,2,1,0:T(8,128)}, f32[4,4,128,128]{3,2,1,0:T(8,128)S(1)}, u32[]{:S(2)}, u32[]{:S(2)}) %collective-permute-start.11) | collective-permute-done | bytes 1048608 | tf_op jit(solution)/shard_map/ppermute | solution.py:25
  206.4 5.0 %gather_fusion.1 = f32[16,4,128,128]{3,2,1,0:T(8,128)} fusion(f32[16,4,128,128]{3,2,1,0:T(8,128)} %constant_dynamic-update-slice_fusion, s32[1024]{0:T(1024)S(1)} %pad_clamp_fusion), kind=kCustom, calls=%fused_computation.1 | custom fusion | bytes 8388672 | tf_op jit(solution)/shard_map/jit(_take)/gather | solution.py:33
  211.5 16.8 %all-gather.7.cloned.1.call-done = f32[4,128,32,128]{3,1,2,0:T(8,128)} async-done(((f32[4,128,2,128]{3,1,2,0:T(8,128)}), f32[4,128,32,128]{3,1,2,0:T(8,128)}) %all-gather.7.cloned.1.call-update) | async-done | bytes 8388624 | tf_op jit(solution)/shard_map/all_gather | solution.py:110
  228.3 6.0 %convolution_bitcast_fusion.1 = f32[4,128,128]{2,1,0:T(8,128)S(1)} fusion(f32[4,128,16,2,128]{4,1,3,2,0:T(8,128)} %bitcast.94, f32[16,2,128,128,1]{3,2,1,0,4:T(8,128)S(1)} %bitcast.99), kind=kOutput, calls=%fused_computation.10 | convolution fusion | flops 1610612736 | bytes 10747904 | tf_op jit(solution)/shard_map/taqcx,qcxb->tab/dot_general | solution.py:13
  234.3 2.2 fusion
  236.5 1.9 copy.91
  238.7 35.6 %reduce-scatter.5.cloned.1.call-done = f32[256,256]{1,0:T(8,128)} async-done(((f32[2048,256]{1,0:T(8,128)}), f32[256,256]{1,0:T(8,128)}) %reduce-scatter.5.cloned.1.call-update) | async-done | bytes 262160 | tf_op jit(solution)/shard_map/reduce_scatter | solution.py:66
  (135 shorter events, 46.2 us)
Async XLA Ops:
  6.5 59.5 %all-gather.5.cloned.1.call-start = ((), (), s32[]{:S(2)}) async-start(), calls=%async_computation.4 | async-start | bytes 4456448 | tf_op jit(solution)/shard_map/all_gather | solution.py:89
  8.7 2.2 copy-start.14
  9.0 2.0 copy-start.12
  9.2 1.8 copy-start.16
  11.9 109.5 %reduce-scatter.3.cloned.1.call-start = ((), (), s32[]{:S(2)}) async-start(), calls=%async_computation.2 | async-start | bytes 2359296 | tf_op jit(solution)/shard_map/reduce_scatter | solution.py:66
  12.7 12.4 %collective-permute-start = (f32[6,128,128]{2,1,0:T(8,128)}, f32[6,128,128]{2,1,0:T(8,128)}, u32[]{:S(2)}, u32[]{:S(2)}) collective-permute-start(f32[6,128,128]{2,1,0:T(8,128)} %pad_maximum_fusion.1), channel_id=1, source_target_pairs={{0,16},{16,32},{32,48},{48,64},{64,80},{80,96},{96,112},{112,0},{1... | collective-permute-start | bytes 1179656 | tf_op jit(solution)/shard_map/ppermute | solution.py:92
  12.7 15.0 %collective-permute-start.1 = (f32[6,128,128]{2,1,0:T(8,128)}, f32[6,128,128]{2,1,0:T(8,128)}, u32[]{:S(2)}, u32[]{:S(2)}) collective-permute-start(f32[6,128,128]{2,1,0:T(8,128)} %pad_maximum_fusion.1), channel_id=1, source_target_pairs={{0,32},{16,48},{32,64},{48,80},{64,96},{80,112},{96,0},{112,16},{1... | collective-permute-start | bytes 1179656 | tf_op jit(solution)/shard_map/ppermute | solution.py:92
  14.3 28.7 %collective-permute-start.2 = (f32[6,128,128]{2,1,0:T(8,128)}, f32[6,128,128]{2,1,0:T(8,128)}, u32[]{:S(2)}, u32[]{:S(2)}) collective-permute-start(f32[6,128,128]{2,1,0:T(8,128)} %pad_maximum_fusion.1), channel_id=1, source_target_pairs={{0,48},{16,64},{32,80},{48,96},{64,112},{80,0},{96,16},{112,32},{1... | collective-permute-start | bytes 1179656 | tf_op jit(solution)/shard_map/ppermute | solution.py:92
  16.5 27.7 %collective-permute-start.3 = (f32[6,128,128]{2,1,0:T(8,128)}, f32[6,128,128]{2,1,0:T(8,128)}, u32[]{:S(2)}, u32[]{:S(2)}) collective-permute-start(f32[6,128,128]{2,1,0:T(8,128)} %pad_maximum_fusion.1), channel_id=1, source_target_pairs={{0,64},{16,80},{32,96},{48,112},{64,0},{80,16},{96,32},{112,48},{1... | collective-permute-start | bytes 1179656 | tf_op jit(solution)/shard_map/ppermute | solution.py:92
  18.5 30.4 %collective-permute-start.4 = (f32[6,128,128]{2,1,0:T(8,128)}, f32[6,128,128]{2,1,0:T(8,128)}, u32[]{:S(2)}, u32[]{:S(2)}) collective-permute-start(f32[6,128,128]{2,1,0:T(8,128)} %pad_maximum_fusion.1), channel_id=1, source_target_pairs={{0,80},{16,96},{32,112},{48,0},{64,16},{80,32},{96,48},{112,64},{1... | collective-permute-start | bytes 1179656 | tf_op jit(solution)/shard_map/ppermute | solution.py:92
  25.1 24.8 %collective-permute-start.5 = (f32[6,128,128]{2,1,0:T(8,128)}, f32[6,128,128]{2,1,0:T(8,128)S(1)}, u32[]{:S(2)}, u32[]{:S(2)}) collective-permute-start(f32[6,128,128]{2,1,0:T(8,128)} %pad_maximum_fusion.1), channel_id=1, source_target_pairs={{0,96},{16,112},{32,0},{48,16},{64,32},{80,48},{96,64},{112,80},{1... | collective-permute-start | bytes 1179656 | tf_op jit(solution)/shard_map/ppermute | solution.py:92
  27.8 23.0 %collective-permute-start.6 = (f32[6,128,128]{2,1,0:T(8,128)}, f32[6,128,128]{2,1,0:T(8,128)S(1)}, u32[]{:S(2)}, u32[]{:S(2)}) collective-permute-start(f32[6,128,128]{2,1,0:T(8,128)} %pad_maximum_fusion.1), channel_id=1, source_target_pairs={{0,112},{16,0},{32,16},{48,32},{64,48},{80,64},{96,80},{112,96},{1... | collective-permute-start | bytes 1179656 | tf_op jit(solution)/shard_map/ppermute | solution.py:92
  50.8 2.6 copy-start.25
  66.1 4.0 %copy-start.4 = (f32[16,128,128]{2,1,0:T(8,128)S(1)}, f32[16,128,128]{2,1,0:T(8,128)}, u32[]{:S(2)}) copy-start(f32[16,128,128]{2,1,0:T(8,128)} %bitcast_multiply_fusion) | copy-start | bytes 3145732
  86.3 38.6 %copy-start.17 = (f32[4]{0:T(128)S(1)}, f32[4]{0:T(128)}, u32[]{:S(2)}) copy-start(f32[4]{0:T(128)} %copy-done.16) | copy-start | bytes 52
  87.8 140.5 %all-gather.7.cloned.1.call-start = ((), (), s32[]{:S(2)}) async-start(), calls=%async_computation.5 | async-start | bytes 8912896 | tf_op jit(solution)/shard_map/all_gather | solution.py:110
  127.1 147.3 %reduce-scatter.5.cloned.1.call-start = ((), (), s32[]{:S(2)}) async-start(), calls=%async_computation.3 | async-start | bytes 2359296 | tf_op jit(solution)/shard_map/reduce_scatter | solution.py:66
  127.1 10.4 %collective-permute-start.7 = (f32[1,4,128,128]{3,2,1,0:T(8,128)S(1)}, f32[1,4,128,128]{3,2,1,0:T(8,128)S(1)}, u32[]{:S(2)}, u32[]{:S(2)}) collective-permute-start(f32[1,4,128,128]{3,2,1,0:T(8,128)S(1)} %bitcast.103), channel_id=1, source_target_pairs={{0,1},{1,2},{2,3},{3,0},{4,5},{5,6},{6,7},{7,4},{8,9},{9,10},{10,1... | collective-permute-start | bytes 786440 | tf_op jit(solution)/shard_map/ppermute | solution.py:25
  128.6 11.7 %collective-permute-start.8 = (f32[1,4,128,128]{3,2,1,0:T(8,128)S(1)}, f32[1,4,128,128]{3,2,1,0:T(8,128)S(1)}, u32[]{:S(2)}, u32[]{:S(2)}) collective-permute-start(f32[1,4,128,128]{3,2,1,0:T(8,128)S(1)} %bitcast.104), channel_id=1, source_target_pairs={{0,2},{1,3},{2,0},{3,1},{4,6},{5,7},{6,4},{7,5},{8,10},{9,11},{10,... | collective-permute-start | bytes 786440 | tf_op jit(solution)/shard_map/ppermute | solution.py:25
  131.4 10.3 %collective-permute-start.9 = (f32[1,4,128,128]{3,2,1,0:T(8,128)S(1)}, f32[1,4,128,128]{3,2,1,0:T(8,128)S(1)}, u32[]{:S(2)}, u32[]{:S(2)}) collective-permute-start(f32[1,4,128,128]{3,2,1,0:T(8,128)S(1)} %bitcast.105), channel_id=1, source_target_pairs={{0,3},{1,0},{2,1},{3,2},{4,7},{5,4},{6,5},{7,6},{8,11},{9,8},{10,9... | collective-permute-start | bytes 786440 | tf_op jit(solution)/shard_map/ppermute | solution.py:25
  137.5 4.2 %copy-start.9 = (f32[1,4,128,128]{3,2,1,0:T(8,128)}, f32[1,4,128,128]{3,2,1,0:T(8,128)S(1)}, u32[]{:S(2)}) copy-start(f32[1,4,128,128]{3,2,1,0:T(8,128)S(1)} %collective-permute-done.7) | copy-start | bytes 786436
  140.3 2.5 copy-start.10
  142.9 31.6 %collective-permute-start.10 = (f32[4,4,128,128]{3,2,1,0:T(8,128)}, f32[4,4,128,128]{3,2,1,0:T(8,128)}, u32[]{:S(2)}, u32[]{:S(2)}) collective-permute-start(f32[4,4,128,128]{3,2,1,0:T(8,128)} %pad_maximum_fusion), channel_id=1, source_target_pairs={{0,4},{1,5},{2,6},{3,7},{4,8},{5,9},{6,10},{7,11},{8,12},{9,13},{1... | collective-permute-start | bytes 3145736 | tf_op jit(solution)/shard_map/ppermute | solution.py:25
  144.7 59.6 %collective-permute-start.11 = (f32[4,4,128,128]{3,2,1,0:T(8,128)}, f32[4,4,128,128]{3,2,1,0:T(8,128)S(1)}, u32[]{:S(2)}, u32[]{:S(2)}) collective-permute-start(f32[4,4,128,128]{3,2,1,0:T(8,128)} %pad_maximum_fusion), channel_id=1, source_target_pairs={{0,8},{1,9},{2,10},{3,11},{4,12},{5,13},{6,14},{7,15},{8,0},{9,1},... | collective-permute-start | bytes 3145736 | tf_op jit(solution)/shard_map/ppermute | solution.py:25
  147.6 57.8 %collective-permute-start.12 = (f32[4,4,128,128]{3,2,1,0:T(8,128)}, f32[4,4,128,128]{3,2,1,0:T(8,128)S(1)}, u32[]{:S(2)}, u32[]{:S(2)}) collective-permute-start(f32[4,4,128,128]{3,2,1,0:T(8,128)} %pad_maximum_fusion), channel_id=1, source_target_pairs={{0,12},{1,13},{2,14},{3,15},{4,0},{5,1},{6,2},{7,3},{8,4},{9,5},{1... | collective-permute-start | bytes 3145736 | tf_op jit(solution)/shard_map/ppermute | solution.py:25
  228.3 6.0 %copy-start = (f32[16,4,128,128]{3,2,1,0:T(8,128)S(1)}, f32[16,4,128,128]{3,2,1,0:T(8,128)}, u32[]{:S(2)}) copy-start(f32[16,4,128,128]{3,2,1,0:T(8,128)} %gather_fusion.1) | copy-start | bytes 12582916
  228.3 6.0 %copy-start.3 = (f32[4,128,2,128]{3,1,2,0:T(8,128)S(1)}, f32[4,128,2,128]{3,1,2,0:T(8,128)}, u32[]{:S(2)}) copy-start(f32[4,128,2,128]{3,1,2,0:T(8,128)} %multiply_multiply_fusion) | copy-start | bytes 1572868
  228.3 6.0 %copy-start.13 = (f32[2]{0:T(128)S(1)}, f32[2]{0:T(128)}, u32[]{:S(2)}) copy-start(f32[2]{0:T(128)} %copy-done.12) | copy-start | bytes 28
  236.5 1.9 copy-start.20
  236.5 39.0 %copy-start.2 = (f32[4,128,2,128]{3,2,1,0:T(2,128)S(1)}, f32[4,128,2,128]{3,2,1,0:T(2,128)}, u32[]{:S(2)}) copy-start(f32[4,128,2,128]{3,2,1,0:T(2,128)} %param.5) | copy-start | bytes 1572868
  236.5 38.9 %copy-start.6 = (f32[4,128,128]{2,1,0:T(8,128)S(1)}, f32[4,128,128]{2,1,0:T(8,128)}, u32[]{:S(2)}) copy-start(f32[4,128,128]{2,1,0:T(8,128)} %copy-done.5) | copy-start | bytes 786436
  236.5 38.9 %copy-start.8 = (f32[2,128,2,128]{3,1,2,0:T(8,128)S(1)}, f32[2,128,2,128]{3,1,2,0:T(8,128)}, u32[]{:S(2)}) copy-start(f32[2,128,2,128]{3,1,2,0:T(8,128)} %copy-done.7) | copy-start | bytes 786436
  (11 other events, 12.3 us)
Sparse Core Ops, SparseCore 0:
  12.0 53.9 all-gather.4
  87.9 33.4 reduce-scatter.2
  127.2 101.0 all-gather.6
  238.6 35.7 reduce-scatter.4
